TPU v7x, 512 devices: a whole 4x8x8 slice. The times are simulated.
512 devices in a mesh: wide: 32 (over z, x), narrow: 16 (over y, core).
Axes of the slice: x: 4, y: 8, z: 8, core: 2. Of those that a mesh axis runs over, the one named last changes fastest.
Arguments:
- tokens: bfloat16 [1024, 16384], P('wide', 'narrow'), may hold values from -200 to 200
- norm_gain: float32 [16384], P('narrow'), may hold values from 0.25 to 1.75
- gate_weight: bfloat16 [26624, 16384], P('wide', 'narrow'), may hold values from -0.046875 to 0.046875
- up_weight: bfloat16 [26624, 16384], P('wide', 'narrow'), may hold values from -0.046875 to 0.046875
- down_weight: bfloat16 [26624, 16384], P('wide', 'narrow'), may hold values from -0.0390625 to 0.0390625
Outputs:
- ffn_out: bfloat16 [1024, 16384], P('wide', 'narrow')
All inputs are finite; a program needn't handle non-finite values.
Results may differ from a plain program's by a relative error of at most 0.03.
Values may be sent and summed in bfloat16 or wider, within the bound.
No kernel may reach another device: no remote copies, remote signals or barrier semaphores. Data moves between devices by JAX's collectives and lax.ppermute only.
A program may use at most 64 MiB of HBM per device.

v0:
```python
import jax
import jax.numpy as jnp
from jax import lax
from jax.sharding import PartitionSpec as P

D = 16384
EPS = 1e-05


def project_pair(rows, gate_weight, up_weight):
    dims = (((1,), (1,)), ((), ()))
    gate = lax.dot_general(rows, gate_weight, dims, preferred_element_type=jnp.float32)
    upward = lax.dot_general(rows, up_weight, dims, preferred_element_type=jnp.float32)
    return jnp.concatenate([gate, upward], axis=1)


def activate(sums, width):
    return (jax.nn.silu(sums[:, :width]) * sums[:, width:]).astype(jnp.bfloat16)


def local(tokens, norm_gain, gate_weight, up_weight, down_weight):
    width = gate_weight.shape[0]
    whole = lax.all_gather(tokens, "wide", axis=0, tiled=True)
    values = whole.astype(jnp.float32)
    squares = lax.psum(jnp.sum(values * values, axis=1), "narrow")
    normed = (values * lax.rsqrt(squares[:, None] / D + EPS) * norm_gain).astype(jnp.bfloat16)
    sums = lax.psum(
        project_pair(normed, gate_weight, up_weight).astype(jnp.bfloat16), "narrow"
    ).astype(jnp.float32)
    hidden = activate(sums, width)
    return lax.psum_scatter(
        jnp.dot(hidden, down_weight, preferred_element_type=jnp.float32).astype(jnp.bfloat16),
        "wide",
        scatter_dimension=0,
        tiled=True,
    )


def solution(mesh):
    in_specs = (
        P("wide", "narrow"),
        P("narrow"),
        P("wide", "narrow"),
        P("wide", "narrow"),
        P("wide", "narrow"),
    )
    out_specs = P("wide", "narrow")
    return jax.shard_map(local, mesh=mesh, in_specs=in_specs, out_specs=out_specs, check_vma=False)
```

profile of v0, /device:TPU:8, one launch (start us, length us, event | category | flops | bytes accessed | tf_op | source)
XLA Modules:
  0.0 490.7 jit_solution(1981325503855157326)
XLA Ops:
  6.5 0.0 copy-start
  6.5 0.0 all-gather.2.cloned.1.call-start
  6.5 0.7 all-gather.2.cloned.1.call-update
  7.3 0.0 all-reduce.2.cloned.1.call-start
  7.3 91.8 %all-gather.2.cloned.1.call-done = bf16[1024,1024]{1,0:T(8,128)(2,1)} async-done(((bf16[32,1024]{1,0:T(8,128)(2,1)}), bf16[1024,1024]{1,0:T(8,128)(2,1)}) %all-gather.2.cloned.1.call-update) | async-done | bytes 2097168 | tf_op jit(solution)/shard_map/all_gather | solution.py:23
  99.1 2.1 fusion
  101.2 20.6 %psum.14 = f32[1024]{0:T(1024)S(1)} all-reduce(f32[1024]{0:T(1024)S(1)} %fusion), channel_id=1, replica_groups=mesh['wide'=32,'narrow'=16] {'narrow'}, use_global_device_ids=true, to_apply=%region_1.0 | all-reduce | flops 1024 | bytes 8192 | tf_op jit(solution)/shard_map/psum | solution.py:25
  121.8 0.0 copy-start.1
  121.8 0.0 copy-start.2
  121.8 0.0 copy-start.3
  121.9 4.3 convolution_convert_fusion.1
  126.2 0.0 copy-done.1
  126.2 0.0 copy-done.2
  126.2 0.0 copy-done.3
  126.2 2.1 convolution_convert_fusion.2
  128.3 2.1 pad_maximum_fusion
  130.4 0.0 all-reduce.2.cloned.1.call-update
  130.4 0.0 reduce-scatter.2.cloned.1.call-start
  130.5 121.9 %all-reduce.2.cloned.1.call-done = bf16[1024,1664]{0,1:T(8,128)(2,1)} async-done(((bf16[1024,1664]{0,1:T(8,128)(2,1)}), bf16[1024,1664]{0,1:T(8,128)(2,1)}) %all-reduce.2.cloned.1.call-update) | async-done | bytes 3407888 | tf_op jit(solution)/shard_map/psum | solution.py:27
  252.4 2.8 convert_element_type.18
  255.2 0.0 copy-done
  255.2 3.9 convolution_convert_fusion
  259.0 0.0 reduce-scatter.2.cloned.1.call-update
  259.1 225.1 %reduce-scatter.2.cloned.1.call-done = bf16[32,1024]{1,0:T(8,128)(2,1)} async-done(((bf16[1024,1024]{1,0:T(8,128)(2,1)}), bf16[32,1024]{1,0:T(8,128)(2,1)}) %reduce-scatter.2.cloned.1.call-update) | async-done | bytes 65552 | tf_op jit(solution)/shard_map/reduce_scatter | solution.py:31
  (1 shorter events, 0.0 us)
Async XLA Ops:
  6.5 248.6 %copy-start = (bf16[832,1024]{1,0:T(8,128)(2,1)S(1)}, bf16[832,1024]{1,0:T(8,128)(2,1)}, u32[]{:S(2)}) copy-start(bf16[832,1024]{1,0:T(8,128)(2,1)} %param.9) | copy-start | bytes 5111812
  6.5 92.6 %all-gather.2.cloned.1.call-start = ((), (), s32[]{:S(2)}) async-start(), calls=%async_computation.1 | async-start | bytes 2162688 | tf_op jit(solution)/shard_map/all_gather | solution.py:23
  7.3 245.1 %all-reduce.2.cloned.1.call-start = ((), (), s32[]{:S(2)}) async-start(), calls=%async_computation.2 | async-start | bytes 6815744 | tf_op jit(solution)/shard_map/psum | solution.py:27
  121.8 4.3 copy-start.1
  121.8 4.3 copy-start.2
  121.8 4.3 copy-start.3
  130.4 353.8 %reduce-scatter.2.cloned.1.call-start = ((), (), s32[]{:S(2)}) async-start(), calls=%async_computation.3 | async-start | bytes 2162688 | tf_op jit(solution)/shard_map/reduce_scatter | solution.py:31
Sparse Core Ops, SparseCore 0:
  10.5 88.5 all-gather.1
  130.6 121.7 all-reduce.1
  259.2 224.9 reduce-scatter.1
where the time goes:
time: 491 us
  waiting for transfers between devices  440 us (90%)
  blocking collectives  20.6 us (4%)
  between operations  13.2 us (3%)
  matrix products  10.3 us (2%)
  other arithmetic  6.94 us (1%)
    reduce_scatter x1, waiting for transfers between devices, local(): lax.psum_scatter(jnp.dot(hidden, down_weight, preferred_element_type=jnp....  225 us
    psum x1, waiting for transfers between devices, local(): lax.psum(project_pair(normed, gate_weight, up_weight).astype(jnp.bfloat16...  122 us
    all_gather x1, waiting for transfers between devices, local(): whole = lax.all_gather(tokens, 'wide', axis=0, tiled=True)  91.8 us
    psum x1, blocking collectives, local(): squares = lax.psum(jnp.sum(values * values, axis=1), 'narrow')  20.6 us
  transfers between devices with their start and end apart: 3, of which 3 were waited for; matrix products, arithmetic and copies ran while one was open for 0% of the time, Pallas kernels for 0%

commit v1 on v0

--- a/solution.py
+++ b/solution.py
@@ -20,7 +20,19 @@
 
 def local(tokens, norm_gain, gate_weight, up_weight, down_weight):
     width = gate_weight.shape[0]
-    whole = lax.all_gather(tokens, "wide", axis=0, tiled=True)
+
+    def detail_modes(dim_at, axis_key, m):
+        total_devices = lax.psum(1, axis_key)
+        carry = lax.all_to_all(
+            jnp.tile(m, [total_devices if b == dim_at else 1 for b in range(m.ndim)]),
+            axis_key,
+            split_axis=dim_at,
+            concat_axis=dim_at,
+            tiled=True,
+        )
+        return carry
+
+    whole = detail_modes(0, "wide", tokens)
     values = whole.astype(jnp.float32)
     squares = lax.psum(jnp.sum(values * values, axis=1), "narrow")
     normed = (values * lax.rsqrt(squares[:, None] / D + EPS) * norm_gain).astype(jnp.bfloat16)

time: 491 us -> 463 us (0.943)
  waiting for transfers between devices: 440 us -> 346 us
  blocking collectives: 20.6 us -> 84.8 us
    all_gather x1 -> x0, waiting for transfers between devices: 91.8 us -> none  [local(): whole = lax.all_gather(tokens, 'wide', axis=0, tiled=True)]
    all_to_all x0 -> x1, blocking collectives: none -> 63.5 us  [detail_modes(): lax.all_to_all(jnp.tile(m, [total_devices if b == dim_at else 1 for b in...]
  transfers between devices with their start and end apart: 3 -> 2, of which waited for: 3 -> 2; matrix products, arithmetic and copies ran while one was open for 0% -> 0% of each run, Pallas kernels for 0% -> 0%
where the time goes in v1:
time: 463 us
  waiting for transfers between devices  346 us (75%)
  blocking collectives  84.8 us (18%)
  between operations  13.5 us (3%)
  matrix products  7.9 us (2%)
  other arithmetic  7.6 us (2%)
    reduce_scatter x1, waiting for transfers between devices, local(): lax.psum_scatter(jnp.dot(hidden, down_weight, preferred_element_type=jnp....  225 us
    psum x1, waiting for transfers between devices, local(): lax.psum(project_pair(normed, gate_weight, up_weight).astype(jnp.bfloat16...  121 us
    all_to_all x1, blocking collectives, detail_modes(): lax.all_to_all(jnp.tile(m, [total_devices if b == dim_at else 1 for b in...  63.5 us
    psum x1, blocking collectives, local(): squares = lax.psum(jnp.sum(values * values, axis=1), 'narrow')  21.2 us
  transfers between devices with their start and end apart: 2, of which 2 were waited for; matrix products, arithmetic and copies ran while one was open for 0% of the time, Pallas kernels for 0%

profile of v1, /device:TPU:8, one launch (start us, length us, event | category | flops | bytes accessed | tf_op | source)
XLA Modules:
  0.0 462.8 jit_solution(7485414060389519266)
XLA Ops:
  6.5 0.0 copy-start
  6.5 0.0 all-reduce.2.cloned.1.call-start
  6.5 1.2 tile.2
  7.8 63.5 %all_to_all.6 = bf16[32,32,1024]{2,1,0:T(8,128)(2,1)S(1)} all-to-all(bf16[32,32,1024]{2,1,0:T(8,128)(2,1)S(1)} %tile.2), channel_id=1, replica_groups=mesh['wide'=32,'narrow'=16] {'wide'}, dimensions={0} | all-to-all | bytes 4194304 | tf_op jit(solution)/shard_map/all_to_all | solution.py:26
  71.3 0.0 copy-start.1
  71.3 1.3 copy-done.1
  72.6 0.0 copy-start.2
  72.6 0.5 multiply_reduce_fusion
  73.1 0.1 reduce_sum.12
  73.2 21.2 %psum.14 = f32[1024]{0:T(1024)S(1)} all-reduce(f32[1024]{0:T(1024)S(1)} %reduce_sum.12), channel_id=1, replica_groups=mesh['wide'=32,'narrow'=16] {'narrow'}, use_global_device_ids=true, to_apply=%region_1.0 | all-reduce | flops 1024 | bytes 8192 | tf_op jit(solution)/shard_map/psum | solution.py:37
  94.4 0.0 copy-done.2
  94.4 0.0 copy-start.3
  94.5 2.3 fusion.1
  96.7 0.0 copy-done.3
  96.7 0.0 copy-start.4
  96.7 2.0 convolution_convert_fusion.1
  98.8 0.0 copy-done.4
  98.8 2.0 convolution_convert_fusion.2
  100.8 2.1 pad_maximum_fusion
  102.9 0.0 all-reduce.2.cloned.1.call-update
  102.9 0.0 reduce-scatter.2.cloned.1.call-start
  103.0 121.4 %all-reduce.2.cloned.1.call-done = bf16[1024,1664]{0,1:T(8,128)(2,1)} async-done(((bf16[1024,1664]{0,1:T(8,128)(2,1)}), bf16[1024,1664]{0,1:T(8,128)(2,1)}) %all-reduce.2.cloned.1.call-update) | async-done | bytes 3407888 | tf_op jit(solution)/shard_map/psum | solution.py:39
  224.3 2.8 convert_element_type.26
  227.1 0.0 copy-done
  227.1 3.9 convolution_convert_fusion
  231.0 0.0 reduce-scatter.2.cloned.1.call-update
  231.0 224.9 %reduce-scatter.2.cloned.1.call-done = bf16[32,1024]{1,0:T(8,128)(2,1)} async-done(((bf16[1024,1024]{1,0:T(8,128)(2,1)}), bf16[32,1024]{1,0:T(8,128)(2,1)}) %reduce-scatter.2.cloned.1.call-update) | async-done | bytes 65552 | tf_op jit(solution)/shard_map/reduce_scatter | solution.py:43
  (1 shorter events, 0.0 us)
Async XLA Ops:
  6.5 220.6 %copy-start = (bf16[832,1024]{1,0:T(8,128)(2,1)S(1)}, bf16[832,1024]{1,0:T(8,128)(2,1)}, u32[]{:S(2)}) copy-start(bf16[832,1024]{1,0:T(8,128)(2,1)} %param.9) | copy-start | bytes 5111812
  6.5 217.8 %all-reduce.2.cloned.1.call-start = ((), (), s32[]{:S(2)}) async-start(), calls=%async_computation.2 | async-start | bytes 6815744 | tf_op jit(solution)/shard_map/psum | solution.py:39
  71.3 1.4 copy-start.1
  72.6 21.8 %copy-start.2 = (f32[1024]{0:T(1024)S(1)}, f32[1024]{0:T(1024)}, u32[]{:S(2)}) copy-start(f32[1024]{0:T(1024)} %param.6) | copy-start | bytes 12292
  94.4 2.3 copy-start.3
  96.7 2.0 copy-start.4
  102.9 353.0 %reduce-scatter.2.cloned.1.call-start = ((), (), s32[]{:S(2)}) async-start(), calls=%async_computation.3 | async-start | bytes 2162688 | tf_op jit(solution)/shard_map/reduce_scatter | solution.py:43
Sparse Core Ops, SparseCore 0:
  103.0 121.2 all-reduce.1
  231.1 224.7 reduce-scatter.1
